TPU v7x, 32 devices: a whole 2x2x4 slice. The times are simulated.
32 devices in a mesh: group: 4 (over z), member: 8 (over y, x, core).
Axes of the slice: x: 2, y: 2, z: 4, core: 2. Of those that a mesh axis runs over, the one named last changes fastest.
Arguments:
- query_feat: bfloat16 [4096, 4096], P(('group', 'member'))
- code_feat: bfloat16 [4096, 4096], P(('group', 'member'))
- projection: bfloat16 [4096, 1024], replicated
- hard_ids: int32 [32, 16], P(('group', 'member')), may hold values from 0 to 63, as said below
- loss_weight: float32 [4096], P(('group', 'member')), may hold values from 1 to 4
Outputs:
- query_grad: bfloat16 [4096, 4096], P(('group', 'member'))
- code_grad: bfloat16 [4096, 4096], P(('group', 'member'))
- projection_grad: float32 [4096, 1024], P(('group', 'member'))
Inputs may be any that keep to these rules, and one draw needn't show every extreme that they name: `hard_ids`: entry (owner device g * 8 + m) * 2 + slot names code rows of that device. A row names 16 different blocks, none of its own group; at most 8 of them lie in one group, and exactly 8 in some group of every row.
All inputs are finite; a program needn't handle non-finite values.
Results may differ from a plain program's by a relative error of at most 0.02.
Values may be sent and summed in bfloat16 or wider, within the bound.
No kernel may reach another device: no remote copies, remote signals or barrier semaphores. Data moves between devices by JAX's collectives and lax.ppermute only.
A program may use at most 128 MiB of HBM per device.

v0:
```python
import jax
import jax.numpy as jnp
from jax import lax
from jax.sharding import PartitionSpec as P

CB = 64
inverse_temp = 120.0
epsilon = 1e-06


def embed(features, projection):
    values = jnp.dot(features, projection, preferred_element_type=jnp.float32)
    inverse = lax.rsqrt(jnp.sum(values * values, axis=1) + epsilon)
    unit_vec = values * inverse[:, None]
    return (unit_vec, inverse, unit_vec.astype(jnp.bfloat16))


def norm_back(upstream, unit_vec, inverse):
    inner_prod = jnp.sum(unit_vec * upstream, axis=1, keepdims=True)
    return (inverse[:, None] * (upstream - unit_vec * inner_prod)).astype(jnp.bfloat16)


def shift_all(x, axis):
    size = lax.axis_size(axis)
    index = lax.axis_index(axis)
    got = [x]
    for s in range(1, size):
        got.append(lax.ppermute(x, axis, [(i, (i + s) % size) for i in range(size)]))
    order = (index - jnp.arange(size)) % size
    return jax.tree.map(lambda *xs: jnp.take(jnp.stack(xs, axis=0), order, axis=0), *got)


def exchange(parts, axis):
    size = lax.axis_size(axis)
    index = lax.axis_index(axis)
    got = [jnp.take(parts, index, axis=0)]
    for s in range(1, size):
        sent = jnp.take(parts, (index + s) % size, axis=0)
        got.append(lax.ppermute(sent, axis, [(i, (i + s) % size) for i in range(size)]))
    stacked = jnp.stack(got, axis=0)
    return jnp.take(stacked, (index - jnp.arange(size)) % size, axis=0)


def body(query_feat, code_feat, projection, hard_ids, loss_weight):
    groups = lax.axis_size("group")
    members = lax.axis_size("member")
    group_index = lax.axis_index("group")
    member_index = lax.axis_index("member")
    queries_dev = query_feat.shape[0]
    feat_width = query_feat.shape[1]
    emb_width = projection.shape[1]
    slot_count = queries_dev // CB
    per_group = members * slot_count
    group_span = members * queries_dev
    rows_dev = feat_width // (groups * members)
    feats = jnp.stack([query_feat, code_feat], axis=0).reshape(
        2, queries_dev, groups, members, rows_dev
    )
    feats = jnp.transpose(feats, (3, 0, 1, 2, 4))
    feat_cols = lax.all_to_all(feats, "member", split_axis=0, concat_axis=0, tiled=True)
    q_unit, q_inv, q_emb = embed(query_feat, projection)
    code_values = lax.all_gather(
        jnp.dot(code_feat, projection, preferred_element_type=jnp.float32),
        "member",
        axis=0,
        tiled=True,
    )
    c_inv = lax.rsqrt(jnp.sum(code_values * code_values, axis=1) + epsilon)
    c_unit = code_values * c_inv[:, None]
    group_codes = c_unit.astype(jnp.bfloat16)
    q_all = lax.all_to_all(
        jnp.broadcast_to(q_emb[None], (groups, queries_dev, emb_width)),
        "group",
        split_axis=0,
        concat_axis=0,
        tiled=True,
    )
    ids_all = shift_all(hard_ids[0], "group")
    block_ids = group_index * per_group + jnp.arange(per_group, dtype=jnp.int32)
    asked = jnp.any(ids_all[:, :, None] == block_ids[None, None, :], axis=1)
    own = jnp.arange(groups, dtype=jnp.int32) == group_index
    block_mask = asked | own[:, None]
    col_mask = jnp.broadcast_to(block_mask[:, :, None], (groups, per_group, CB)).reshape(
        groups, 1, group_span
    )
    scores = inverse_temp * jnp.einsum(
        "gqe,ke->gqk", q_all, group_codes, preferred_element_type=jnp.float32
    )
    scores = jnp.where(col_mask, scores, -jnp.inf)
    part_max = jnp.max(scores, axis=2)
    safe_max = jnp.where(part_max > -jnp.inf, part_max, 0.0)
    part_sum = jnp.sum(jnp.exp(scores - safe_max[:, :, None]), axis=2)
    weights_row = jnp.broadcast_to(loss_weight[None], (groups, queries_dev))
    stats = shift_all(jnp.stack([part_max, part_sum, weights_row], axis=0), "group")
    w_all = stats[:, 2, 0]
    row_max = jnp.max(stats[:, 0], axis=0)
    row_sum = jnp.sum(stats[:, 1] * jnp.exp(stats[:, 0] - row_max[None]), axis=0)
    log_total = row_max + jnp.log(row_sum)
    offsets = jnp.arange(queries_dev, dtype=jnp.int32)
    columns = jnp.arange(group_span, dtype=jnp.int32)
    positive = (columns[None, :] == (member_index * queries_dev + offsets)[:, None]).astype(
        jnp.float32
    )
    positive = positive[None] * own[:, None, None].astype(jnp.float32)
    factor = w_all * inverse_temp
    grad = (factor[:, :, None] * (jnp.exp(scores - log_total[:, :, None]) - positive)).astype(
        jnp.bfloat16
    )
    code_terms = None
    for g in range(groups):
        term = jnp.dot(grad[g].T, q_all[g], preferred_element_type=jnp.float32)
        term = jnp.where(g == group_index, term, term.astype(jnp.bfloat16).astype(jnp.float32))
        code_terms = term if code_terms is None else code_terms + term
    code_sum = code_terms.astype(jnp.bfloat16)
    grad_dq, code_sum = lax.optimization_barrier((grad, code_sum))
    code_delta = lax.psum(code_sum, "member").astype(jnp.float32)
    delta_parts = jnp.einsum(
        "gqk,ke->gqe", grad_dq, group_codes, preferred_element_type=jnp.float32
    )
    returned = exchange(delta_parts.astype(jnp.bfloat16), "group").astype(jnp.float32)
    own_part = jnp.take(delta_parts, group_index, axis=0)
    query_delta = own_part + jnp.sum(jnp.where(own[:, None, None], 0.0, returned), axis=0)
    dz_query = norm_back(query_delta, q_unit, q_inv)
    dz_code_all = norm_back(code_delta, c_unit, c_inv)
    dz_code = lax.dynamic_slice_in_dim(dz_code_all, member_index * queries_dev, queries_dev, 0)
    query_grad = jnp.einsum(
        "qe,de->qd", dz_query, projection, preferred_element_type=jnp.float32
    ).astype(jnp.bfloat16)
    code_grad = jnp.einsum(
        "qe,de->qd", dz_code, projection, preferred_element_type=jnp.float32
    ).astype(jnp.bfloat16)
    dzq_all = lax.all_to_all(
        jnp.broadcast_to(dz_query[None], (members, queries_dev, emb_width)),
        "member",
        split_axis=0,
        concat_axis=0,
        tiled=True,
    )
    dzc_all = dz_code_all.reshape(members, queries_dev, emb_width)
    proj_parts = jnp.einsum(
        "mqgr,mqe->gre", feat_cols[:, 0], dzq_all, preferred_element_type=jnp.float32
    ) + jnp.einsum("mqgr,mqe->gre", feat_cols[:, 1], dzc_all, preferred_element_type=jnp.float32)
    own_proj = jnp.take(proj_parts, group_index, axis=0)
    sent_proj = jnp.where(own[:, None, None], 0.0, proj_parts).astype(jnp.bfloat16)
    projection_grad = own_proj + lax.psum_scatter(
        sent_proj, "group", scatter_dimension=0, tiled=True
    ).reshape(rows_dev, emb_width).astype(jnp.float32)
    return (query_grad, code_grad, projection_grad)


def solution(mesh):
    return jax.shard_map(
        body,
        mesh=mesh,
        in_specs=(
            P(("group", "member"), None),
            P(("group", "member"), None),
            P(),
            P(("group", "member"), None),
            P(("group", "member")),
        ),
        out_specs=(
            P(("group", "member"), None),
            P(("group", "member"), None),
            P(("group", "member"), None),
        ),
        check_vma=False,
    )
```

profile of v0, /device:TPU:0, one launch (start us, length us, event | category | flops | bytes accessed | tf_op | source)
XLA Modules:
  0.0 204.6 jit_solution(2245639925189366476)
XLA Ops:
  7.2 5.8 %fusion.26 = f32[128,1024]{1,0:T(8,128)} fusion(bf16[128,4096]{1,0:T(8,128)(2,1)} %param.10, bf16[4096,1024]{1,0:T(8,128)(2,1)} %param.11), kind=kOutput, calls=%fused_computation.91 | convolution fusion | flops 1073741824 | bytes 9961472 | tf_op jit(solution)/shard_map/dot_general | solution.py:63
  13.1 3.1 %collective-permute-start = (s32[16]{0:T(128)S(1)}, s32[16]{0:T(128)S(1)}, u32[]{:S(2)}, u32[]{:S(2)}) collective-permute-start(s32[16]{0:T(128)S(1)} %bitcast.128), channel_id=1, source_target_pairs={{0,8},{8,16},{16,24},{24,0},{1,9},{9,17},{17,25},{25,1},{2,10},{10... | collective-permute-start | bytes 200 | tf_op jit(solution)/shard_map/ppermute | solution.py:28
  16.2 2.6 %collective-permute-start.1 = (s32[16]{0:T(128)S(1)}, s32[16]{0:T(128)S(1)}, u32[]{:S(2)}, u32[]{:S(2)}) collective-permute-start(s32[16]{0:T(128)S(1)} %bitcast.129), channel_id=1, source_target_pairs={{0,16},{8,24},{16,0},{24,8},{1,17},{9,25},{17,1},{25,9},{2,18},{10... | collective-permute-start | bytes 200 | tf_op jit(solution)/shard_map/ppermute | solution.py:28
  18.8 1.4 collective-permute-start.2
  20.2 5.0 %multiply_reduce_fusion.2 = (f32[128]{0:T(128)S(1)}, f32[128,1024]{1,0:T(8,128)S(1)}) fusion(bf16[128,4096]{1,0:T(8,128)(2,1)S(1)} %copy-done.5, bf16[4096,1024]{1,0:T(8,128)(2,1)} %param.11), kind=kOutput, calls=%fused_computation.31 | convolution fusion | flops 1074003840 | bytes 9961984 | tf_op jit(solution)/shard_map/dot_general | solution.py:12
  25.2 0.1 multiply_convert_fusion.3
  25.3 1.1 broadcast_in_dim.126
  26.4 3.6 %all-to-all-start = ((bf16[4,128,1024]{2,1,0:T(8,128)(2,1)}), bf16[4,128,1024]{2,1,0:T(8,128)(2,1)S(1)}, u32[]{:S(2)}, u32[]{:S(2)}) async-start(bf16[4,128,1024]{2,1,0:T(8,128)(2,1)} %broadcast_in_dim.126), calls=%async_computation | async-start | bytes 2097152 | tf_op jit(solution)/shard_map/all_to_all | solution.py:71
  30.1 1.3 copy.23
  31.4 1.3 copy.24
  32.8 1.4 maximum_bitcast_fusion
  34.2 0.9 fusion.6
  35.1 1.5 copy.25
  36.6 0.6 gather_fusion
  37.1 0.1 broadcast_select_fusion.1
  37.2 0.1 compare_reduce_fusion
  37.3 0.1 broadcast_or_fusion
  37.4 0.1 broadcast_in_dim.123
  37.4 0.1 broadcast_in_dim.124
  37.5 15.0 %all-gather.2.cloned.1.call-done = f32[1024,1024]{1,0:T(8,128)} async-done(((f32[128,1024]{1,0:T(8,128)}), f32[1024,1024]{1,0:T(8,128)}) %all-gather.2.cloned.1.call-update) | async-done | bytes 4194320 | tf_op jit(solution)/shard_map/all_gather | solution.py:62
  52.6 2.5 %multiply_reduce_fusion = f32[1024]{0:T(1024)S(1)} fusion(f32[1024,1024]{1,0:T(8,128)} %all-gather.2.cloned.1.call-done), kind=kLoop, calls=%fused_computation.11 | loop fusion | flops 2096128 | bytes 4198400 | tf_op jit(solution)/shard_map/reduce_sum | solution.py:68
  55.1 4.4 %all-to-all-start.1 = ((bf16[8,2,128,4,128]{2,4,3,1,0:T(8,128)(2,1)}), bf16[8,2,128,4,128]{2,4,3,1,0:T(8,128)(2,1)}, u32[]{:S(2)}, u32[]{:S(2)}) async-start(bf16[8,2,128,4,128]{2,4,3,1,0:T(8,128)(2,1)} %copy.25), calls=%async_computation.1 | async-start | bytes 4194304 | tf_op jit(solution)/shard_map/all_to_all | solution.py:60
  59.5 3.6 %fusion.24 = (f32[4,128]{1,0:T(4,128)S(1)}, f32[4,128,1024]{2,1,0:T(8,128)S(1)}) fusion(bf16[4,128,1024]{2,1,0:T(8,128)(2,1)S(1)} %all-to-all-done, f32[1024,1024]{1,0:T(8,128)} %all-gather.2.cloned.1.call-done, f32[1024]{0:T(1024)S(1)} %add_rsqrt_fusion, pred[4,1024]{1,0:T(4,128)(4,1)S(1)} %broadcast_in_dim.124), kind=kOutput, calls=%fused_computation.89 | convolution fusion | flops 1077411328 | bytes 7350272 | tf_op jit(solution)/shard_map/gqe,ke->gqk/dot_general | solution.py:86
  63.2 0.5 exponential_reduce_fusion
  63.7 0.2 copy-done.8
  63.8 2.5 %collective-permute-start.4 = (f32[3,4,128]{2,1,0:T(4,128)S(1)}, f32[3,4,128]{2,1,0:T(4,128)S(1)}, u32[]{:S(2)}, u32[]{:S(2)}) collective-permute-start(f32[3,4,128]{2,1,0:T(4,128)S(1)} %get-tuple-element.38), channel_id=1, source_target_pairs={{0,16},{8,24},{16,0},{24,8},{1,17},{9,25},{17,1},{25,9},{2,18},{10... | collective-permute-start | bytes 18440 | tf_op jit(solution)/shard_map/ppermute | solution.py:28
  66.3 1.4 collective-permute-start.5
  67.7 0.6 collective-permute-start.3
  68.3 0.1 collective-permute-done.4
  68.4 1.5 collective-permute-done.5
  69.9 3.2 %collective-permute-done.3 = f32[3,4,128]{2,1,0:T(4,128)S(1)} collective-permute-done((f32[3,4,128]{2,1,0:T(4,128)S(1)}, f32[3,4,128]{2,1,0:T(4,128)S(1)}, u32[]{:S(2)}, u32[]{:S(2)}) %collective-permute-start.3) | collective-permute-done | bytes 6176 | tf_op jit(solution)/shard_map/ppermute | solution.py:28
  73.2 0.6 gather_fusion.1
  73.8 0.1 broadcast_select_fusion
  73.9 1.6 multiply_convert_fusion.1
  75.5 0.7 fusion.11
  76.2 0.7 fusion.12
  76.9 0.7 fusion.10
  77.7 2.4 %add_convert_fusion = bf16[1024,1024]{1,0:T(8,128)(2,1)} fusion(f32[1024,1024]{1,0:T(8,128)S(1)} %fusion.10, f32[1024,1024]{1,0:T(8,128)S(1)} %fusion.11, f32[1024,1024]{1,0:T(8,128)S(1)} %fusion.12, pred[]{:T(512)S(6)} %eq.75, pred[]{:T(512)S(6)} %eq.74, pred[]{:T(512)S(6)} %eq.73, pred[]{:T(512)S(6)} %eq.72, bf16[4,128,1024]{2,1,0:T(8,128)(2,1)S(1)} %all-to-all-done, ...), kind=kOutput, calls=%fused_computation.10 | convolution fusion | flops 285212672 | bytes 15204356 | tf_op jit(solution)/shard_map/dot_general | solution.py:111
  80.1 3.8 %fusion.25 = (bf16[4,128,1024]{2,1,0:T(8,128)(2,1)S(1)}, f32[4,128,1024]{2,1,0:T(8,128)S(1)}) fusion(bf16[4,128,1024]{2,1,0:T(8,128)(2,1)} %copy-done.1, f32[1024,1024]{1,0:T(8,128)} %all-gather.2.cloned.1.call-done, f32[1024]{0:T(1024)S(1)} %add_rsqrt_fusion), kind=kOutput, calls=%fused_computation.90 | convolution fusion | flops 1076363264 | bytes 8392704 | tf_op jit(solution)/shard_map/gqk,ke->gqe/dot_general | solution.py:117
  83.9 0.9 dynamic-slice_select_fusion
  84.9 0.6 collective-permute-start.7
  85.4 3.3 %collective-permute-start.8 = (bf16[128,1024]{1,0:T(8,128)(2,1)}, bf16[128,1024]{1,0:T(8,128)(2,1)S(1)}, u32[]{:S(2)}, u32[]{:S(2)}) collective-permute-start(bf16[128,1024]{1,0:T(8,128)(2,1)} %get-tuple-element.34), channel_id=1, source_target_pairs={{0,24},{8,0},{16,8},{24,16},{1,25},{9,1},{17,9},{25,17},{2,26},{10... | collective-permute-start | bytes 786440 | tf_op jit(solution)/shard_map/ppermute | solution.py:39
  88.7 7.4 %collective-permute-done.6 = bf16[128,1024]{1,0:T(8,128)(2,1)S(1)} collective-permute-done((bf16[128,1024]{1,0:T(8,128)(2,1)}, bf16[128,1024]{1,0:T(8,128)(2,1)S(1)}, u32[]{:S(2)}, u32[]{:S(2)}) %collective-permute-start.6) | collective-permute-done | bytes 262176 | tf_op jit(solution)/shard_map/ppermute | solution.py:39
  96.2 8.9 %collective-permute-done.7 = bf16[128,1024]{1,0:T(8,128)(2,1)S(1)} collective-permute-done((bf16[128,1024]{1,0:T(8,128)(2,1)}, bf16[128,1024]{1,0:T(8,128)(2,1)S(1)}, u32[]{:S(2)}, u32[]{:S(2)}) %collective-permute-start.7) | collective-permute-done | bytes 262176 | tf_op jit(solution)/shard_map/ppermute | solution.py:39
  105.1 1.1 pad_maximum_fusion
  106.2 2.9 %gather_fusion.2 = bf16[4,128,1024]{2,1,0:T(8,128)(2,1)} fusion(bf16[4,128,1024]{2,1,0:T(8,128)(2,1)} %pad_maximum_fusion, s32[1024]{0:T(1024)S(1)} %pad_clamp_fusion), kind=kCustom, calls=%fused_computation.2 | custom fusion | bytes 2097168 | tf_op jit(solution)/shard_map/jit(_take)/gather | solution.py:41
  109.1 1.6 select_reduce_fusion
  110.7 0.2 multiply_reduce_fusion.1
  110.9 0.2 multiply_convert_fusion.2
  111.1 1.6 broadcast_in_dim.134
  112.7 4.3 %all-to-all-start.2 = ((bf16[8,128,1024]{2,1,0:T(8,128)(2,1)}), bf16[8,128,1024]{2,1,0:T(8,128)(2,1)}, u32[]{:S(2)}, u32[]{:S(2)}) async-start(bf16[8,128,1024]{2,1,0:T(8,128)(2,1)} %broadcast_in_dim.134), calls=%async_computation.2 | async-start | bytes 4194304 | tf_op jit(solution)/shard_map/all_to_all | solution.py:132
  117.1 0.0 reduce-scatter.2.cloned.1.call-start
  117.1 2.8 %fusion.23 = (bf16[8,1,128,4,128]{2,4,3,1,0:T(8,128)(2,1)S(1)}, bf16[8,1,128,4,128]{2,4,3,1,0:T(8,128)(2,1)}) fusion(bf16[8,2,128,4,128]{2,4,3,1,0:T(8,128)(2,1)} %all-to-all-done.1), kind=kLoop, calls=%fused_computation.88 | loop fusion | bytes 4194304 | tf_op jit(solution)/shard_map/slice | solution.py:142
  119.9 37.8 %all-reduce.2.cloned.1.call-done = bf16[1024,1024]{1,0:T(8,128)(2,1)} async-done(((bf16[1024,1024]{1,0:T(8,128)(2,1)}), bf16[1024,1024]{1,0:T(8,128)(2,1)}) %all-reduce.2.cloned.1.call-update) | async-done | bytes 2097168 | tf_op jit(solution)/shard_map/psum | solution.py:116
  157.7 3.7 %fusion = f32[1024]{0:T(1024)S(1)} fusion(bf16[1024,1024]{1,0:T(8,128)(2,1)} %all-reduce.2.cloned.1.call-done, f32[1024,1024]{1,0:T(8,128)} %all-gather.2.cloned.1.call-done, f32[1024]{0:T(1024)S(1)} %add_rsqrt_fusion), kind=kLoop, calls=%fused_computation.7 | loop fusion | flops 4193280 | bytes 6299648 | tf_op jit(solution)/shard_map/reduce_sum | solution.py:19
  161.3 0.4 copy-done
  161.7 0.7 copy-done.2
  162.4 0.8 fusion.2
  163.2 3.2 %fusion.4 = f32[4,128,1024,1]{2,1,3,0:T(8,128)S(1)} fusion(bf16[8,128,1024]{2,1,0:T(8,128)(2,1)} %all-to-all-done.2, bf16[8,1,128,4,128]{2,4,3,1,0:T(8,128)(2,1)} %get-tuple-element.32), kind=kOutput, calls=%fused_computation.16 | convolution fusion | flops 1073741824 | bytes 5242880 | tf_op jit(solution)/shard_map/mqgr,mqe->gre/dot_general | solution.py:140
  166.4 2.9 %select_convert_fusion = (bf16[4,128,1024]{2,1,0:T(8,128)(2,1)}, f32[4,128,1024]{2,1,0:T(8,128)}) fusion(pred[4]{0:T(512)(128)(4,1)S(1)} %iota_compare_fusion.1, bf16[8,128,1024,1]{2,1,0,3:T(8,128)(2,1)S(1)} %bitcast.116, bf16[8,1,128,4,128]{2,4,3,1,0:T(8,128)(2,1)S(1)} %get-tuple-element.31, f32[4,128,1024,1]{2,1,3,0:T(8,128)S(1)} %fusion.4), kind=kOutput, calls=%fused_computation.18 | convolution fusion | flops 1074790400 | bytes 8388612 | tf_op jit(solution)/shard_map/mqgr,mqe->gre/dot_general | solution.py:142
  169.3 7.2 %convolution_convert_fusion.1 = bf16[128,4096]{1,0:T(8,128)(2,1)} fusion(bf16[128,1024]{1,0:T(8,128)(2,1)S(1)} %multiply_convert_fusion.2, bf16[4096,1024]{1,0:T(8,128)(2,1)} %param.11), kind=kOutput, calls=%fused_computation.6 | convolution fusion | flops 1074266112 | bytes 9699328 | tf_op jit(solution)/shard_map/qe,de->qd/dot_general | solution.py:126
  176.6 7.2 %convolution_convert_fusion = bf16[128,4096]{1,0:T(8,128)(2,1)} fusion(bf16[4096,1024]{1,0:T(8,128)(2,1)} %param.11, bf16[1024,1024]{1,0:T(8,128)(2,1)S(1)} %fusion.2, s32[]{:T(128)S(6)} %select_n.153), kind=kOutput, calls=%fused_computation.5 | convolution fusion | flops 1074266112 | bytes 9699332 | tf_op jit(solution)/shard_map/qe,de->qd/dot_general | solution.py:129
  183.8 12.3 %reduce-scatter.2.cloned.1.call-done = bf16[1,128,1024]{2,1,0:T(8,128)(2,1)} async-done(((bf16[4,128,1024]{2,1,0:T(8,128)(2,1)}), bf16[1,128,1024]{2,1,0:T(8,128)(2,1)}) %reduce-scatter.2.cloned.1.call-update) | async-done | bytes 262160 | tf_op jit(solution)/shard_map/reduce_scatter | solution.py:145
  196.1 2.0 convert_add_fusion
  (48 shorter events, 0.3 us)
Async XLA Ops:
  7.2 5.9 %copy-start.9 = (s32[1,16]{1,0:T(1,128)S(1)}, s32[1,16]{1,0:T(1,128)}, u32[]{:S(2)}) copy-start(s32[1,16]{1,0:T(1,128)} %param.12) | copy-start | bytes 196
  7.2 13.0 %copy-start.5 = (bf16[128,4096]{1,0:T(8,128)(2,1)S(1)}, bf16[128,4096]{1,0:T(8,128)(2,1)}, u32[]{:S(2)}) copy-start(bf16[128,4096]{1,0:T(8,128)(2,1)} %param.9) | copy-start | bytes 3145732
  7.2 45.4 %all-gather.2.cloned.1.call-start = ((), (), s32[]{:S(2)}) async-start(), calls=%async_computation.4 | async-start | bytes 4718592 | tf_op jit(solution)/shard_map/all_gather | solution.py:62
  13.1 23.4 %collective-permute-start = (s32[16]{0:T(128)S(1)}, s32[16]{0:T(128)S(1)}, u32[]{:S(2)}, u32[]{:S(2)}) collective-permute-start(s32[16]{0:T(128)S(1)} %bitcast.128), channel_id=1, source_target_pairs={{0,8},{8,16},{16,24},{24,0},{1,9},{9,17},{17,25},{25,1},{2,10},{10... | collective-permute-start | bytes 200 | tf_op jit(solution)/shard_map/ppermute | solution.py:28
  16.2 20.3 %collective-permute-start.1 = (s32[16]{0:T(128)S(1)}, s32[16]{0:T(128)S(1)}, u32[]{:S(2)}, u32[]{:S(2)}) collective-permute-start(s32[16]{0:T(128)S(1)} %bitcast.129), channel_id=1, source_target_pairs={{0,16},{8,24},{16,0},{24,8},{1,17},{9,25},{17,1},{25,9},{2,18},{10... | collective-permute-start | bytes 200 | tf_op jit(solution)/shard_map/ppermute | solution.py:28
  18.8 17.7 %collective-permute-start.2 = (s32[16]{0:T(128)S(1)}, s32[16]{0:T(128)S(1)}, u32[]{:S(2)}, u32[]{:S(2)}) collective-permute-start(s32[16]{0:T(128)S(1)} %bitcast.130), channel_id=1, source_target_pairs={{0,24},{8,0},{16,8},{24,16},{1,25},{9,1},{17,9},{25,17},{2,26},{10... | collective-permute-start | bytes 200 | tf_op jit(solution)/shard_map/ppermute | solution.py:28
  25.1 1.2 copy-start.3
  26.4 5.1 %copy-start.6 = (bf16[128,4096]{1,0:T(8,128)(2,1)S(1)}, bf16[128,4096]{1,0:T(8,128)(2,1)}, u32[]{:S(2)}) copy-start(bf16[128,4096]{1,0:T(8,128)(2,1)} %param.10) | copy-start | bytes 3145732
  26.4 28.7 %all-to-all-start = ((bf16[4,128,1024]{2,1,0:T(8,128)(2,1)}), bf16[4,128,1024]{2,1,0:T(8,128)(2,1)S(1)}, u32[]{:S(2)}, u32[]{:S(2)}) async-start(bf16[4,128,1024]{2,1,0:T(8,128)(2,1)} %broadcast_in_dim.126), calls=%async_computation | async-start | bytes 2097152 | tf_op jit(solution)/shard_map/all_to_all | solution.py:71
  31.4 1.3 copy-start.7
  55.1 56.0 %all-to-all-start.1 = ((bf16[8,2,128,4,128]{2,4,3,1,0:T(8,128)(2,1)}), bf16[8,2,128,4,128]{2,4,3,1,0:T(8,128)(2,1)}, u32[]{:S(2)}, u32[]{:S(2)}) async-start(bf16[8,2,128,4,128]{2,4,3,1,0:T(8,128)(2,1)} %copy.25), calls=%async_computation.1 | async-start | bytes 4194304 | tf_op jit(solution)/shard_map/all_to_all | solution.py:60
  59.5 98.2 %all-reduce.2.cloned.1.call-start = ((), (), s32[]{:S(2)}) async-start(), calls=%async_computation.5 | async-start | bytes 4194304 | tf_op jit(solution)/shard_map/psum | solution.py:116
  63.2 0.7 copy-start.8
  63.8 4.6 %collective-permute-start.4 = (f32[3,4,128]{2,1,0:T(4,128)S(1)}, f32[3,4,128]{2,1,0:T(4,128)S(1)}, u32[]{:S(2)}, u32[]{:S(2)}) collective-permute-start(f32[3,4,128]{2,1,0:T(4,128)S(1)} %get-tuple-element.38), channel_id=1, source_target_pairs={{0,16},{8,24},{16,0},{24,8},{1,17},{9,25},{17,1},{25,9},{2,18},{10... | collective-permute-start | bytes 18440 | tf_op jit(solution)/shard_map/ppermute | solution.py:28
  66.3 3.6 %collective-permute-start.5 = (f32[3,4,128]{2,1,0:T(4,128)S(1)}, f32[3,4,128]{2,1,0:T(4,128)S(1)}, u32[]{:S(2)}, u32[]{:S(2)}) collective-permute-start(f32[3,4,128]{2,1,0:T(4,128)S(1)} %get-tuple-element.38), channel_id=1, source_target_pairs={{0,24},{8,0},{16,8},{24,16},{1,25},{9,1},{17,9},{25,17},{2,26},{10... | collective-permute-start | bytes 18440 | tf_op jit(solution)/shard_map/ppermute | solution.py:28
  67.7 5.4 %collective-permute-start.3 = (f32[3,4,128]{2,1,0:T(4,128)S(1)}, f32[3,4,128]{2,1,0:T(4,128)S(1)}, u32[]{:S(2)}, u32[]{:S(2)}) collective-permute-start(f32[3,4,128]{2,1,0:T(4,128)S(1)} %get-tuple-element.38), channel_id=1, source_target_pairs={{0,8},{8,16},{16,24},{24,0},{1,9},{9,17},{17,25},{25,1},{2,10},{10... | collective-permute-start | bytes 18440 | tf_op jit(solution)/shard_map/ppermute | solution.py:28
  75.5 2.2 %copy-start.1 = (bf16[4,128,1024]{2,1,0:T(8,128)(2,1)}, bf16[4,128,1024]{2,1,0:T(8,128)(2,1)S(1)}, u32[]{:S(2)}) copy-start(bf16[4,128,1024]{2,1,0:T(8,128)(2,1)S(1)} %multiply_convert_fusion.1) | copy-start | bytes 3145732
  84.9 11.3 %collective-permute-start.6 = (bf16[128,1024]{1,0:T(8,128)(2,1)}, bf16[128,1024]{1,0:T(8,128)(2,1)S(1)}, u32[]{:S(2)}, u32[]{:S(2)}) collective-permute-start(bf16[128,1024]{1,0:T(8,128)(2,1)} %get-tuple-element.36), channel_id=1, source_target_pairs={{0,8},{8,16},{16,24},{24,0},{1,9},{9,17},{17,25},{25,1},{2,10},{10... | collective-permute-start | bytes 786440 | tf_op jit(solution)/shard_map/ppermute | solution.py:39
  84.9 20.2 %collective-permute-start.7 = (bf16[128,1024]{1,0:T(8,128)(2,1)}, bf16[128,1024]{1,0:T(8,128)(2,1)S(1)}, u32[]{:S(2)}, u32[]{:S(2)}) collective-permute-start(bf16[128,1024]{1,0:T(8,128)(2,1)} %get-tuple-element.35), channel_id=1, source_target_pairs={{0,16},{8,24},{16,0},{24,8},{1,17},{9,25},{17,1},{25,9},{2,18},{10... | collective-permute-start | bytes 786440 | tf_op jit(solution)/shard_map/ppermute | solution.py:39
  85.4 19.6 %collective-permute-start.8 = (bf16[128,1024]{1,0:T(8,128)(2,1)}, bf16[128,1024]{1,0:T(8,128)(2,1)S(1)}, u32[]{:S(2)}, u32[]{:S(2)}) collective-permute-start(bf16[128,1024]{1,0:T(8,128)(2,1)} %get-tuple-element.34), channel_id=1, source_target_pairs={{0,24},{8,0},{16,8},{24,16},{1,25},{9,1},{17,9},{25,17},{2,26},{10... | collective-permute-start | bytes 786440 | tf_op jit(solution)/shard_map/ppermute | solution.py:39
  106.2 4.5 %copy-start.4 = (f32[128,1024]{1,0:T(8,128)S(1)}, f32[128,1024]{1,0:T(8,128)}, u32[]{:S(2)}) copy-start(f32[128,1024]{1,0:T(8,128)} %copy-done.3) | copy-start | bytes 1572868
  112.7 50.5 %all-to-all-start.2 = ((bf16[8,128,1024]{2,1,0:T(8,128)(2,1)}), bf16[8,128,1024]{2,1,0:T(8,128)(2,1)}, u32[]{:S(2)}, u32[]{:S(2)}) async-start(bf16[8,128,1024]{2,1,0:T(8,128)(2,1)} %broadcast_in_dim.134), calls=%async_computation.2 | async-start | bytes 4194304 | tf_op jit(solution)/shard_map/all_to_all | solution.py:132
  117.1 79.1 %reduce-scatter.2.cloned.1.call-start = ((), (), s32[]{:S(2)}) async-start(), calls=%async_computation.6 | async-start | bytes 1310720 | tf_op jit(solution)/shard_map/reduce_scatter | solution.py:145
  157.7 4.0 %copy-start = (f32[1024,1024]{1,0:T(8,128)S(1)}, f32[1024,1024]{1,0:T(8,128)}, u32[]{:S(2)}) copy-start(f32[1024,1024]{1,0:T(8,128)} %all-gather.2.cloned.1.call-done) | copy-start | bytes 12582916
  157.7 4.7 %copy-start.2 = (bf16[1024,1024]{1,0:T(8,128)(2,1)S(1)}, bf16[1024,1024]{1,0:T(8,128)(2,1)}, u32[]{:S(2)}) copy-start(bf16[1024,1024]{1,0:T(8,128)(2,1)} %all-reduce.2.cloned.1.call-done) | copy-start | bytes 6291460
Sparse Core Ops, SparseCore 0:
  13.2 39.2 all-gather.1
  88.8 68.7 all-reduce.1
  169.5 26.6 reduce-scatter.1
where the time goes:
time: 205 us
  waiting for transfers between devices  86.3 us (42%)
  matrix products  43.5 us (21%)
  starting transfers between devices  27.8 us (14%)
  other arithmetic  17.9 us (9%)
  local copies, waits for them, and re-layouts  15 us (7%)
  between operations  14 us (7%)
    psum x1, waiting for transfers between devices, body(): code_delta = lax.psum(code_sum, 'member').astype(jnp.float32)  37.8 us
    ppermute x3, waiting for transfers between devices, exchange(): lax.ppermute(sent, axis, [(i, (i + s) % size) for i in range(size)])  16.4 us
    all_gather x1, waiting for transfers between devices, body(): lax.all_gather(jnp.dot(code_feat, projection, preferred_element_type=jnp....  15 us
    reduce_scatter x1, waiting for transfers between devices, body(): lax.psum_scatter(sent_proj, 'group', scatter_dimension=0, tiled=True)  12.3 us
    ppermute x6, starting transfers between devices, shift_all(): lax.ppermute(x, axis, [(i, (i + s) % size) for i in range(size)])  11.5 us
    dot_general x1, matrix products, body(): jnp.einsum('qe,de->qd', dz_query, projection, preferred_element_type=jnp....  7.24 us
    dot_general x1, matrix products, body(): jnp.einsum('qe,de->qd', dz_code, projection, preferred_element_type=jnp.f...  7.24 us
    dot_general x1, matrix products, body(): jnp.dot(code_feat, projection, preferred_element_type=jnp.float32)  5.85 us
  transfers between devices with their start and end apart: 15, of which 8 were waited for; matrix products, arithmetic and copies ran while one was open for 30% of the time, Pallas kernels for 0%

commit v1 on v0

--- a/solution.py
+++ b/solution.py
@@ -6,6 +6,18 @@
 CB = 64
 inverse_temp = 120.0
 epsilon = 1e-06
+
+
+def doubled_up(array, axis, dim):
+    ways, here, step = (lax.axis_size(axis), lax.axis_index(axis), array.shape[dim])
+    line, have = (array, 1)
+    while have < ways:
+        line = jnp.concatenate(
+            [line, lax.ppermute(line, axis, [(d, (d - have) % ways) for d in range(ways)])],
+            axis=dim,
+        )
+        have = 2 * have
+    return jnp.roll(line, here * step, axis=dim)
 
 
 def embed(features, projection):
@@ -59,11 +71,8 @@
     feats = jnp.transpose(feats, (3, 0, 1, 2, 4))
     feat_cols = lax.all_to_all(feats, "member", split_axis=0, concat_axis=0, tiled=True)
     q_unit, q_inv, q_emb = embed(query_feat, projection)
-    code_values = lax.all_gather(
-        jnp.dot(code_feat, projection, preferred_element_type=jnp.float32),
-        "member",
-        axis=0,
-        tiled=True,
+    code_values = doubled_up(
+        jnp.dot(code_feat, projection, preferred_element_type=jnp.float32), "member", 0
     )
     c_inv = lax.rsqrt(jnp.sum(code_values * code_values, axis=1) + epsilon)
     c_unit = code_values * c_inv[:, None]

time: 205 us -> 308 us (1.50)
  waiting for transfers between devices: 86.3 us -> 166 us
  local copies, waits for them, and re-layouts: 15 us -> 25.5 us
  other arithmetic: 17.9 us -> 24 us
  starting transfers between devices: 27.8 us -> 31.6 us
    ppermute x0 -> x3, waiting for transfers between devices: none -> 54.9 us  [doubled_up(): lax.ppermute(line, axis, [(d, (d - have) % ways) for d in range(ways)])]
    psum x1, waiting for transfers between devices: 37.8 us -> 77.6 us  [body(): code_delta = lax.psum(code_sum, 'member').astype(jnp.float32)]
    all_gather x1 -> x0, waiting for transfers between devices: 15 us -> none  [body(): lax.all_gather(jnp.dot(code_feat, projection, preferred_element_type=jnp....]
    unnamed x22 -> x26, local copies, waits for them, and re-layouts: 3.84 us -> 12.9 us
    ppermute x0 -> x3, starting transfers between devices: none -> 4.4 us  [doubled_up(): lax.ppermute(line, axis, [(d, (d - have) % ways) for d in range(ways)])]
    dot_general x4, matrix products: 4.6 us -> 8.38 us  [body(): term = jnp.dot(grad[g].T, q_all[g], preferred_element_type=jnp.float32)]
    dot_general x1, matrix products: 4.98 us -> 1.42 us  [embed(): values = jnp.dot(features, projection, preferred_element_type=jnp.float32)]
    convert_element_type x2, other arithmetic: 0.98 us -> 4.22 us  [norm_back(): (inverse[:, None] * (upstream - unit_vec * inner_prod)).astype(jnp.bfloat16)]
  transfers between devices with their start and end apart: 15 -> 17, of which waited for: 8 -> 9; matrix products, arithmetic and copies ran while one was open for 30% -> 25% of each run, Pallas kernels for 0% -> 0%
where the time goes in v1:
time: 308 us; the launch traced here: 307 us
  waiting for transfers between devices  166 us (54%)
  matrix products  45.1 us (15%)
  starting transfers between devices  31.6 us (10%)
  local copies, waits for them, and re-layouts  25.5 us (8%)
  other arithmetic  24 us (8%)
  between operations  14.3 us (5%)
    psum x1, waiting for transfers between devices, body(): code_delta = lax.psum(code_sum, 'member').astype(jnp.float32)  77.6 us
    ppermute x3, waiting for transfers between devices, doubled_up(): lax.ppermute(line, axis, [(d, (d - have) % ways) for d in range(ways)])  54.9 us
    ppermute x3, waiting for transfers between devices, exchange(): lax.ppermute(sent, axis, [(i, (i + s) % size) for i in range(size)])  16.2 us
    unnamed x26, local copies, waits for them, and re-layouts  12.9 us
    reduce_scatter x1, waiting for transfers between devices, body(): lax.psum_scatter(sent_proj, 'group', scatter_dimension=0, tiled=True)  12 us
    ppermute x6, starting transfers between devices, shift_all(): lax.ppermute(x, axis, [(i, (i + s) % size) for i in range(size)])  10.2 us
    dot_general x4, matrix products, body(): term = jnp.dot(grad[g].T, q_all[g], preferred_element_type=jnp.float32)  8.38 us
    dot_general x1, matrix products, body(): jnp.einsum('qe,de->qd', dz_code, projection, preferred_element_type=jnp.f...  7.24 us
  transfers between devices with their start and end apart: 17, of which 9 were waited for; matrix products, arithmetic and copies ran while one was open for 25% of the time, Pallas kernels for 0%

profile of v1, /device:TPU:0, one launch (start us, length us, event | category | flops | bytes accessed | tf_op | source)
XLA Modules:
  0.0 306.9 jit_solution(4779380462408494592)
XLA Ops:
  7.2 5.9 %constant_dynamic-update-slice_fusion.7 = (f32[2048,1024]{1,0:T(8,128)}, f32[128,1024]{1,0:T(8,128)S(1)}) fusion(bf16[128,4096]{1,0:T(8,128)(2,1)} %param.10, bf16[4096,1024]{1,0:T(8,128)(2,1)} %param.11), kind=kOutput, calls=%fused_computation.63 | convolution fusion | flops 1073741824 | bytes 10485760 | tf_op jit(solution)/shard_map/dot_general | solution.py:75
  13.1 3.4 %collective-permute-start.3 = (f32[128,1024]{1,0:T(8,128)S(1)}, f32[128,1024]{1,0:T(8,128)S(1)}, u32[]{:S(2)}, u32[]{:S(2)}) collective-permute-start(f32[128,1024]{1,0:T(8,128)S(1)} %get-tuple-element.42), channel_id=1, source_target_pairs={{0,7},{1,0},{2,1},{3,2},{4,3},{5,4},{6,5},{7,6},{8,15},{9,8},{10,9... | collective-permute-start | bytes 1572872 | tf_op jit(solution)/shard_map/ppermute | solution.py:16
  16.5 6.7 %collective-permute-done.3 = f32[128,1024]{1,0:T(8,128)S(1)} collective-permute-done((f32[128,1024]{1,0:T(8,128)S(1)}, f32[128,1024]{1,0:T(8,128)S(1)}, u32[]{:S(2)}, u32[]{:S(2)}) %collective-permute-start.3) | collective-permute-done | bytes 524320 | tf_op jit(solution)/shard_map/ppermute | solution.py:16
  23.2 0.6 collective-permute-start.4
  23.8 1.6 collective-permute-start
  25.4 2.6 collective-permute-start.1
  28.0 1.3 collective-permute-start.2
  29.4 1.4 multiply_reduce_fusion.2
  30.8 18.0 %collective-permute-done.4 = f32[256,1024]{1,0:T(8,128)S(1)} collective-permute-done((f32[256,1024]{1,0:T(8,128)S(1)}, f32[256,1024]{1,0:T(8,128)S(1)}, u32[]{:S(2)}, u32[]{:S(2)}) %collective-permute-start.4) | collective-permute-done | bytes 1048608 | tf_op jit(solution)/shard_map/ppermute | solution.py:16
  48.9 1.5 pad_maximum_fusion
  50.9 1.1 broadcast_in_dim.126
  52.0 4.9 %all-to-all-start = ((bf16[4,128,1024]{2,1,0:T(8,128)(2,1)}), bf16[4,128,1024]{2,1,0:T(8,128)(2,1)}, u32[]{:S(2)}, u32[]{:S(2)}) async-start(bf16[4,128,1024]{2,1,0:T(8,128)(2,1)} %broadcast_in_dim.126), calls=%async_computation | async-start | bytes 2097152 | tf_op jit(solution)/shard_map/all_to_all | solution.py:80
  56.9 2.3 copy.23
  59.2 1.3 copy.24
  60.5 1.7 maximum_bitcast_fusion
  62.2 1.5 copy.25
  63.8 0.9 fusion.7
  64.7 0.6 gather_fusion
  65.7 0.8 constant_dynamic-update-slice_fusion.6
  66.5 1.1 constant_dynamic-update-slice_fusion.5
  67.7 30.2 %collective-permute-done.5 = f32[512,1024]{1,0:T(8,128)} collective-permute-done((f32[512,1024]{1,0:T(8,128)}, f32[512,1024]{1,0:T(8,128)}, u32[]{:S(2)}, u32[]{:S(2)}) %collective-permute-start.5) | collective-permute-done | bytes 2097184 | tf_op jit(solution)/shard_map/ppermute | solution.py:16
  97.9 3.1 %constant_dynamic-update-slice_fusion.4 = f32[2048,1024]{1,0:T(8,128)} fusion(f32[2048,1024]{1,0:T(8,128)} %constant_dynamic-update-slice_fusion.5, f32[512,1024]{1,0:T(8,128)} %collective-permute-done.5), kind=kLoop, calls=%fused_computation.60 | loop fusion | bytes 4194304
  101.0 0.8 constant_dynamic-update-slice_fusion.3
  101.9 0.8 constant_dynamic-update-slice_fusion.2
  102.7 1.1 constant_dynamic-update-slice_fusion.1
  103.8 3.2 %constant_dynamic-update-slice_fusion = f32[2048,1024]{1,0:T(8,128)} fusion(f32[2048,1024]{1,0:T(8,128)} %constant_dynamic-update-slice_fusion.1, f32[512,1024]{1,0:T(8,128)} %collective-permute-done.5), kind=kLoop, calls=%fused_computation.56 | loop fusion | bytes 4194304 | tf_op jit(solution)/shard_map/jit(_roll_dynamic)/concatenate | solution.py:20
  107.0 2.5 multiply_reduce_fusion
  109.6 3.6 %all-to-all-start.1 = ((bf16[8,2,128,4,128]{2,4,3,1,0:T(8,128)(2,1)}), bf16[8,2,128,4,128]{2,4,3,1,0:T(8,128)(2,1)S(1)}, u32[]{:S(2)}, u32[]{:S(2)}) async-start(bf16[8,2,128,4,128]{2,4,3,1,0:T(8,128)(2,1)} %copy.25), calls=%async_computation.1 | async-start | bytes 4194304 | tf_op jit(solution)/shard_map/all_to_all | solution.py:72
  113.2 4.0 %fusion.27 = (f32[4,128]{1,0:T(4,128)S(1)}, f32[4,128,1024]{2,1,0:T(8,128)S(1)}) fusion(bf16[4,128,1024]{2,1,0:T(8,128)(2,1)} %all-to-all-done, f32[2048,1024]{1,0:T(8,128)} %constant_dynamic-update-slice_fusion, s32[]{:T(128)S(6)} %select_n.150, f32[1024]{0:T(1024)S(1)} %add_rsqrt_fusion, pred[4,1024]{1,0:T(4,128)(4,1)S(1)} %broadcast_in_dim.124), kind=kOutput, calls=%fused_computation.102 | convolution fusion | flops 1077411328 | bytes 7350276 | tf_op jit(solution)/shard_map/gqe,ke->gqk/dot_general | solution.py:95
  117.2 1.3 copy-done.3
  119.1 2.7 collective-permute-start.7
  121.7 1.3 collective-permute-start.8
  123.1 0.7 collective-permute-start.6
  123.7 1.6 collective-permute-done.8
  125.3 3.1 %collective-permute-done.6 = f32[3,4,128]{2,1,0:T(4,128)S(1)} collective-permute-done((f32[3,4,128]{2,1,0:T(4,128)S(1)}, f32[3,4,128]{2,1,0:T(4,128)S(1)}, u32[]{:S(2)}, u32[]{:S(2)}) %collective-permute-start.6) | collective-permute-done | bytes 6176 | tf_op jit(solution)/shard_map/ppermute | solution.py:40
  128.5 0.6 gather_fusion.1
  129.2 2.2 multiply_convert_fusion
  131.4 1.7 fusion.12
  133.1 1.7 fusion.13
  134.8 1.7 fusion.11
  136.5 3.4 %add_convert_fusion = bf16[1024,1024]{1,0:T(8,128)(2,1)} fusion(f32[1024,1024]{1,0:T(8,128)S(1)} %fusion.11, f32[1024,1024]{1,0:T(8,128)S(1)} %fusion.12, f32[1024,1024]{1,0:T(8,128)S(1)} %fusion.13, pred[]{:T(512)S(6)} %eq.78, pred[]{:T(512)S(6)} %eq.77, pred[]{:T(512)S(6)} %eq.76, pred[]{:T(512)S(6)} %eq.75, bf16[4,128,1024]{2,1,0:T(8,128)(2,1)} %all-to-all-done, ...), kind=kOutput, calls=%fused_computation.10 | convolution fusion | flops 285212672 | bytes 15204356 | tf_op jit(solution)/shard_map/dot_general | solution.py:120
  139.8 4.8 %fusion.28 = (bf16[4,128,1024]{2,1,0:T(8,128)(2,1)S(1)}, f32[4,128,1024]{2,1,0:T(8,128)}) fusion(bf16[4,128,1024]{2,1,0:T(8,128)(2,1)S(1)} %multiply_convert_fusion, f32[2048,1024]{1,0:T(8,128)} %constant_dynamic-update-slice_fusion, s32[]{:T(128)S(6)} %select_n.150, f32[1024]{0:T(1024)S(1)} %add_rsqrt_fusion), kind=kOutput, calls=%fused_computation.103 | convolution fusion | flops 1076363264 | bytes 8392708 | tf_op jit(solution)/shard_map/gqk,ke->gqe/dot_general | solution.py:126
  144.8 0.5 collective-permute-start.10
  145.4 3.3 %collective-permute-start.11 = (bf16[128,1024]{1,0:T(8,128)(2,1)S(1)}, bf16[128,1024]{1,0:T(8,128)(2,1)S(1)}, u32[]{:S(2)}, u32[]{:S(2)}) collective-permute-start(bf16[128,1024]{1,0:T(8,128)(2,1)S(1)} %get-tuple-element.34), channel_id=1, source_target_pairs={{0,24},{8,0},{16,8},{24,16},{1,25},{9,1},{17,9},{25,17},{2,26},{10... | collective-permute-start | bytes 786440 | tf_op jit(solution)/shard_map/ppermute | solution.py:51
  148.6 7.2 %collective-permute-done.9 = bf16[128,1024]{1,0:T(8,128)(2,1)S(1)} collective-permute-done((bf16[128,1024]{1,0:T(8,128)(2,1)S(1)}, bf16[128,1024]{1,0:T(8,128)(2,1)S(1)}, u32[]{:S(2)}, u32[]{:S(2)}) %collective-permute-start.9) | collective-permute-done | bytes 262176 | tf_op jit(solution)/shard_map/ppermute | solution.py:51
  155.9 9.0 %collective-permute-done.10 = bf16[128,1024]{1,0:T(8,128)(2,1)S(1)} collective-permute-done((bf16[128,1024]{1,0:T(8,128)(2,1)S(1)}, bf16[128,1024]{1,0:T(8,128)(2,1)S(1)}, u32[]{:S(2)}, u32[]{:S(2)}) %collective-permute-start.10) | collective-permute-done | bytes 262176 | tf_op jit(solution)/shard_map/ppermute | solution.py:51
  164.9 1.1 pad_maximum_fusion.2
  166.0 2.8 gather_fusion.2
  168.8 1.6 select_reduce_fusion
  170.4 1.2 multiply_reduce_fusion.1
  171.7 1.2 multiply_convert_fusion.1
  172.9 1.6 broadcast_in_dim.134
  174.5 4.4 %all-to-all-start.2 = ((bf16[8,128,1024]{2,1,0:T(8,128)(2,1)}), bf16[8,128,1024]{2,1,0:T(8,128)(2,1)}, u32[]{:S(2)}, u32[]{:S(2)}) async-start(bf16[8,128,1024]{2,1,0:T(8,128)(2,1)} %broadcast_in_dim.134), calls=%async_computation.2 | async-start | bytes 4194304 | tf_op jit(solution)/shard_map/all_to_all | solution.py:141
  178.9 0.7 all-reduce.2.cloned.1.call-update
  179.9 1.2 fusion.26
  181.1 77.6 %all-reduce.2.cloned.1.call-done = bf16[1024,1024]{1,0:T(8,128)(2,1)} async-done(((bf16[1024,1024]{1,0:T(8,128)(2,1)}), bf16[1024,1024]{1,0:T(8,128)(2,1)}) %all-reduce.2.cloned.1.call-update) | async-done | bytes 2097168 | tf_op jit(solution)/shard_map/psum | solution.py:125
  258.7 3.7 %fusion = f32[1024]{0:T(1024)S(1)} fusion(bf16[1024,1024]{1,0:T(8,128)(2,1)} %all-reduce.2.cloned.1.call-done, f32[2048,1024]{1,0:T(8,128)} %constant_dynamic-update-slice_fusion, s32[]{:T(128)S(6)} %select_n.150, f32[1024]{0:T(1024)S(1)} %add_rsqrt_fusion), kind=kLoop, calls=%fused_computation.7 | loop fusion | flops 4193280 | bytes 6299652 | tf_op jit(solution)/shard_map/reduce_sum | solution.py:31
  262.4 3.0 fusion.2
  265.4 3.2 %fusion.5 = f32[4,128,1024,1]{2,1,3,0:T(8,128)S(1)} fusion(bf16[8,128,1024]{2,1,0:T(8,128)(2,1)} %all-to-all-done.2, bf16[8,1,128,4,128]{2,4,3,1,0:T(8,128)(2,1)} %get-tuple-element.32), kind=kOutput, calls=%fused_computation.18 | convolution fusion | flops 1073741824 | bytes 5242880 | tf_op jit(solution)/shard_map/mqgr,mqe->gre/dot_general | solution.py:149
  268.6 2.9 select_convert_fusion
  271.5 7.2 %convolution_convert_fusion.1 = bf16[128,4096]{1,0:T(8,128)(2,1)} fusion(bf16[128,1024]{1,0:T(8,128)(2,1)S(1)} %multiply_convert_fusion.1, bf16[4096,1024]{1,0:T(8,128)(2,1)} %param.11), kind=kOutput, calls=%fused_computation.6 | convolution fusion | flops 1074266112 | bytes 9699328 | tf_op jit(solution)/shard_map/qe,de->qd/dot_general | solution.py:135
  278.8 7.2 %convolution_convert_fusion = bf16[128,4096]{1,0:T(8,128)(2,1)} fusion(bf16[4096,1024]{1,0:T(8,128)(2,1)} %param.11, bf16[1024,1024]{1,0:T(8,128)(2,1)S(1)} %fusion.2, s32[]{:T(128)S(6)} %select_n.167), kind=kOutput, calls=%fused_computation.5 | convolution fusion | flops 1074266112 | bytes 9699332 | tf_op jit(solution)/shard_map/qe,de->qd/dot_general | solution.py:138
  286.0 12.0 %reduce-scatter.2.cloned.1.call-done = bf16[1,128,1024]{2,1,0:T(8,128)(2,1)} async-done(((bf16[4,128,1024]{2,1,0:T(8,128)(2,1)}), bf16[1,128,1024]{2,1,0:T(8,128)(2,1)}) %reduce-scatter.2.cloned.1.call-update) | async-done | bytes 262160 | tf_op jit(solution)/shard_map/reduce_scatter | solution.py:154
  298.1 2.0 convert_add_fusion
  (58 shorter events, 2.3 us)
Async XLA Ops:
  7.2 22.2 %copy-start = (bf16[4096,1024]{1,0:T(8,128)(2,1)S(1)}, bf16[4096,1024]{1,0:T(8,128)(2,1)}, u32[]{:S(2)}) copy-start(bf16[4096,1024]{1,0:T(8,128)(2,1)} %param.11) | copy-start | bytes 25165828
  7.2 16.7 %copy-start.8 = (s32[1,16]{1,0:T(1,128)S(1)}, s32[1,16]{1,0:T(1,128)}, u32[]{:S(2)}) copy-start(s32[1,16]{1,0:T(1,128)} %param.12) | copy-start | bytes 196
  7.2 22.2 %copy-start.6 = (bf16[128,4096]{1,0:T(8,128)(2,1)S(1)}, bf16[128,4096]{1,0:T(8,128)(2,1)}, u32[]{:S(2)}) copy-start(bf16[128,4096]{1,0:T(8,128)(2,1)} %param.9) | copy-start | bytes 3145732
  13.1 10.1 %collective-permute-start.3 = (f32[128,1024]{1,0:T(8,128)S(1)}, f32[128,1024]{1,0:T(8,128)S(1)}, u32[]{:S(2)}, u32[]{:S(2)}) collective-permute-start(f32[128,1024]{1,0:T(8,128)S(1)} %get-tuple-element.42), channel_id=1, source_target_pairs={{0,7},{1,0},{2,1},{3,2},{4,3},{5,4},{6,5},{7,6},{8,15},{9,8},{10,9... | collective-permute-start | bytes 1572872 | tf_op jit(solution)/shard_map/ppermute | solution.py:16
  23.2 25.6 %collective-permute-start.4 = (f32[256,1024]{1,0:T(8,128)S(1)}, f32[256,1024]{1,0:T(8,128)S(1)}, u32[]{:S(2)}, u32[]{:S(2)}) collective-permute-start(f32[256,1024]{1,0:T(8,128)S(1)} %pad_maximum_fusion.1), channel_id=1, source_target_pairs={{0,6},{1,7},{2,0},{3,1},{4,2},{5,3},{6,4},{7,5},{8,14},{9,15},{10,... | collective-permute-start | bytes 3145736 | tf_op jit(solution)/shard_map/ppermute | solution.py:16
  23.8 40.9 %collective-permute-start = (s32[16]{0:T(128)S(1)}, s32[16]{0:T(128)S(1)}, u32[]{:S(2)}, u32[]{:S(2)}) collective-permute-start(s32[16]{0:T(128)S(1)} %bitcast.128), channel_id=1, source_target_pairs={{0,8},{8,16},{16,24},{24,0},{1,9},{9,17},{17,25},{25,1},{2,10},{10... | collective-permute-start | bytes 200 | tf_op jit(solution)/shard_map/ppermute | solution.py:40
  25.4 39.3 %collective-permute-start.1 = (s32[16]{0:T(128)S(1)}, s32[16]{0:T(128)S(1)}, u32[]{:S(2)}, u32[]{:S(2)}) collective-permute-start(s32[16]{0:T(128)S(1)} %bitcast.129), channel_id=1, source_target_pairs={{0,16},{8,24},{16,0},{24,8},{1,17},{9,25},{17,1},{25,9},{2,18},{10... | collective-permute-start | bytes 200 | tf_op jit(solution)/shard_map/ppermute | solution.py:40
  28.0 36.7 %collective-permute-start.2 = (s32[16]{0:T(128)S(1)}, s32[16]{0:T(128)S(1)}, u32[]{:S(2)}, u32[]{:S(2)}) collective-permute-start(s32[16]{0:T(128)S(1)} %bitcast.130), channel_id=1, source_target_pairs={{0,24},{8,0},{16,8},{24,16},{1,25},{9,1},{17,9},{25,17},{2,26},{10... | collective-permute-start | bytes 200 | tf_op jit(solution)/shard_map/ppermute | solution.py:40
  30.8 20.0 %copy-start.4 = (f32[128,1024]{1,0:T(8,128)}, f32[128,1024]{1,0:T(8,128)S(1)}, u32[]{:S(2)}) copy-start(f32[128,1024]{1,0:T(8,128)S(1)} %get-tuple-element.40) | copy-start | bytes 1572868
  50.4 8.8 %copy-start.1 = (bf16[128,4096]{1,0:T(8,128)(2,1)S(1)}, bf16[128,4096]{1,0:T(8,128)(2,1)}, u32[]{:S(2)}) copy-start(bf16[128,4096]{1,0:T(8,128)(2,1)} %param.10) | copy-start | bytes 3145732
  50.4 47.5 %collective-permute-start.5 = (f32[512,1024]{1,0:T(8,128)}, f32[512,1024]{1,0:T(8,128)}, u32[]{:S(2)}, u32[]{:S(2)}) collective-permute-start(f32[512,1024]{1,0:T(8,128)} %pad_maximum_fusion), channel_id=1, source_target_pairs={{0,4},{1,5},{2,6},{3,7},{4,0},{5,1},{6,2},{7,3},{8,12},{9,13},{10,... | collective-permute-start | bytes 6291464 | tf_op jit(solution)/shard_map/ppermute | solution.py:16
  52.0 57.6 %all-to-all-start = ((bf16[4,128,1024]{2,1,0:T(8,128)(2,1)}), bf16[4,128,1024]{2,1,0:T(8,128)(2,1)}, u32[]{:S(2)}, u32[]{:S(2)}) async-start(bf16[4,128,1024]{2,1,0:T(8,128)(2,1)} %broadcast_in_dim.126), calls=%async_computation | async-start | bytes 2097152 | tf_op jit(solution)/shard_map/all_to_all | solution.py:80
  109.6 63.3 %all-to-all-start.1 = ((bf16[8,2,128,4,128]{2,4,3,1,0:T(8,128)(2,1)}), bf16[8,2,128,4,128]{2,4,3,1,0:T(8,128)(2,1)S(1)}, u32[]{:S(2)}, u32[]{:S(2)}) async-start(bf16[8,2,128,4,128]{2,4,3,1,0:T(8,128)(2,1)} %copy.25), calls=%async_computation.1 | async-start | bytes 4194304 | tf_op jit(solution)/shard_map/all_to_all | solution.py:72
  113.2 5.8 %copy-start.7 = (f32[128]{0:T(128)S(1)}, f32[128]{0:T(128)}, u32[]{:S(2)}) copy-start(f32[128]{0:T(128)} %param.13) | copy-start | bytes 1540
  117.2 1.3 copy-start.3
  119.1 4.7 %collective-permute-start.7 = (f32[3,4,128]{2,1,0:T(4,128)S(1)}, f32[3,4,128]{2,1,0:T(4,128)S(1)}, u32[]{:S(2)}, u32[]{:S(2)}) collective-permute-start(f32[3,4,128]{2,1,0:T(4,128)S(1)} %get-tuple-element.38), channel_id=1, source_target_pairs={{0,16},{8,24},{16,0},{24,8},{1,17},{9,25},{17,1},{25,9},{2,18},{10... | collective-permute-start | bytes 18440 | tf_op jit(solution)/shard_map/ppermute | solution.py:40
  121.7 3.6 %collective-permute-start.8 = (f32[3,4,128]{2,1,0:T(4,128)S(1)}, f32[3,4,128]{2,1,0:T(4,128)S(1)}, u32[]{:S(2)}, u32[]{:S(2)}) collective-permute-start(f32[3,4,128]{2,1,0:T(4,128)S(1)} %get-tuple-element.38), channel_id=1, source_target_pairs={{0,24},{8,0},{16,8},{24,16},{1,25},{9,1},{17,9},{25,17},{2,26},{10... | collective-permute-start | bytes 18440 | tf_op jit(solution)/shard_map/ppermute | solution.py:40
  123.1 5.4 %collective-permute-start.6 = (f32[3,4,128]{2,1,0:T(4,128)S(1)}, f32[3,4,128]{2,1,0:T(4,128)S(1)}, u32[]{:S(2)}, u32[]{:S(2)}) collective-permute-start(f32[3,4,128]{2,1,0:T(4,128)S(1)} %get-tuple-element.38), channel_id=1, source_target_pairs={{0,8},{8,16},{16,24},{24,0},{1,9},{9,17},{17,25},{25,1},{2,10},{10... | collective-permute-start | bytes 18440 | tf_op jit(solution)/shard_map/ppermute | solution.py:40
  144.7 25.8 %copy-start.5 = (f32[128,1024]{1,0:T(8,128)S(1)}, f32[128,1024]{1,0:T(8,128)}, u32[]{:S(2)}) copy-start(f32[128,1024]{1,0:T(8,128)} %copy-done.4) | copy-start | bytes 1572868
  144.8 11.1 %collective-permute-start.9 = (bf16[128,1024]{1,0:T(8,128)(2,1)S(1)}, bf16[128,1024]{1,0:T(8,128)(2,1)S(1)}, u32[]{:S(2)}, u32[]{:S(2)}) collective-permute-start(bf16[128,1024]{1,0:T(8,128)(2,1)S(1)} %get-tuple-element.36), channel_id=1, source_target_pairs={{0,8},{8,16},{16,24},{24,0},{1,9},{9,17},{17,25},{25,1},{2,10},{10... | collective-permute-start | bytes 786440 | tf_op jit(solution)/shard_map/ppermute | solution.py:51
  144.8 20.0 %collective-permute-start.10 = (bf16[128,1024]{1,0:T(8,128)(2,1)S(1)}, bf16[128,1024]{1,0:T(8,128)(2,1)S(1)}, u32[]{:S(2)}, u32[]{:S(2)}) collective-permute-start(bf16[128,1024]{1,0:T(8,128)(2,1)S(1)} %get-tuple-element.35), channel_id=1, source_target_pairs={{0,16},{8,24},{16,0},{24,8},{1,17},{9,25},{17,1},{25,9},{2,18},{10... | collective-permute-start | bytes 786440 | tf_op jit(solution)/shard_map/ppermute | solution.py:51
  145.4 19.5 %collective-permute-start.11 = (bf16[128,1024]{1,0:T(8,128)(2,1)S(1)}, bf16[128,1024]{1,0:T(8,128)(2,1)S(1)}, u32[]{:S(2)}, u32[]{:S(2)}) collective-permute-start(bf16[128,1024]{1,0:T(8,128)(2,1)S(1)} %get-tuple-element.34), channel_id=1, source_target_pairs={{0,24},{8,0},{16,8},{24,16},{1,25},{9,1},{17,9},{25,17},{2,26},{10... | collective-permute-start | bytes 786440 | tf_op jit(solution)/shard_map/ppermute | solution.py:51
  174.5 90.9 %all-to-all-start.2 = ((bf16[8,128,1024]{2,1,0:T(8,128)(2,1)}), bf16[8,128,1024]{2,1,0:T(8,128)(2,1)}, u32[]{:S(2)}, u32[]{:S(2)}) async-start(bf16[8,128,1024]{2,1,0:T(8,128)(2,1)} %broadcast_in_dim.134), calls=%async_computation.2 | async-start | bytes 4194304 | tf_op jit(solution)/shard_map/all_to_all | solution.py:141
  178.9 79.8 %all-reduce.2.cloned.1.call-start = ((), (), s32[]{:S(2)}) async-start(), calls=%async_computation.4 | async-start | bytes 4194304 | tf_op jit(solution)/shard_map/psum | solution.py:125
  179.6 118.4 %reduce-scatter.2.cloned.1.call-start = ((), (), s32[]{:S(2)}) async-start(), calls=%async_computation.5 | async-start | bytes 1310720 | tf_op jit(solution)/shard_map/reduce_scatter | solution.py:154
  258.7 3.7 %copy-start.2 = (bf16[1024,1024]{1,0:T(8,128)(2,1)S(1)}, bf16[1024,1024]{1,0:T(8,128)(2,1)}, u32[]{:S(2)}) copy-start(bf16[1024,1024]{1,0:T(8,128)(2,1)} %all-reduce.2.cloned.1.call-done) | copy-start | bytes 6291460
Sparse Core Ops, SparseCore 0:
  182.9 75.6 all-reduce.1
  271.7 26.3 reduce-scatter.1
